TPU v7x, 256 devices: a whole 4x4x8 slice. The times are simulated.
256 devices in a mesh: ctx: 32 (over y_lo, z, core), tp: 8 (over y_hi, x).
Axes of the slice: x: 4, y: 4 (y_hi: 2, y_lo: 2; y = y_hi * 2 + y_lo), z: 8, core: 2. Of those that a mesh axis runs over, the one named last changes fastest.
Arguments:
- queries: bfloat16 [4096, 8192], P('ctx', 'tp'), may hold values from -32 to 32
- key_proj: bfloat16 [4096, 1024], P('ctx', 'tp'), may hold values from -12.5 to 12.5
- value_proj: bfloat16 [4096, 1024], P('ctx', 'tp'), may hold values from -6 to 6
- grad_out: bfloat16 [4096, 8192], P('ctx', 'tp'), may hold values from -6 to 6
- key_weight: bfloat16 [8192, 1024], P(None, 'tp'), may hold values from -0.1875 to 0.1875
- value_weight: bfloat16 [8192, 1024], P(None, 'tp'), may hold values from -0.1875 to 0.1875
- doc_start: int32 [4096], P('ctx'), may hold values from 0 to 4095, as said below
Outputs:
- grad_query: bfloat16 [4096, 8192], P('ctx', 'tp')
- grad_key: bfloat16 [4096, 1024], P('ctx', 'tp')
- grad_value: bfloat16 [4096, 1024], P('ctx', 'tp')
- grad_input: bfloat16 [4096, 8192], P('ctx', 'tp')
Inputs may be any that keep to these rules, and one draw needn't show every extreme that they name: doc_start[p] is the first position of the document holding p; documents are runs of consecutive positions, each of 1 to 2048 positions; the first document has exactly 2048 positions and the last position is a document of its own.
All inputs are finite; a program needn't handle non-finite values.
Results may differ from a plain program's by a relative error of at most 0.034.
Values may be sent and summed in bfloat16 or wider, within the bound.
No kernel may reach another device: no remote copies, remote signals or barrier semaphores. Data moves between devices by JAX's collectives and lax.ppermute only.
A program may use at most 64 MiB of HBM per device.

v0:
```python
import math

import jax
import jax.numpy as jnp
from jax import lax
from jax.sharding import PartitionSpec as P

HEADS = 64
KV_HEADS = 8
HD = 128


NEGATIVE = -1e30


def from_behind(value, axis, steps):
    count = lax.axis_size(axis)
    pairs = [(source, (source + steps) % count) for source in range(count)]
    return lax.ppermute(value, axis, pairs)


def block_scores(query_four, keys_three, query_pos, query_first, block_index, tok_rows, soft_scale):
    key_pos = block_index * tok_rows + jnp.arange(tok_rows, dtype=jnp.int32)
    visible = (key_pos[None, :] <= query_pos[:, None]) & (key_pos[None, :] >= query_first[:, None])
    scores = (
        jnp.einsum("qkgd,pkd->kgqp", query_four, keys_three, preferred_element_type=jnp.float32)
        * soft_scale
    )
    return jnp.where(visible, scores, NEGATIVE)


def shards(queries, key_proj, value_proj, grad_out, key_weight, value_weight, doc_start):
    tok_rows = queries.shape[0]
    heads_kv = key_proj.shape[1] // HD
    kv_cols = key_proj.shape[1]
    group_size = HEADS // KV_HEADS
    soft_scale = 1.0 / math.sqrt(HD)
    cycle_size = lax.axis_size("ctx")
    my_index = lax.axis_index("ctx")
    start_keys, start_values = (key_proj, value_proj)
    query_four = queries.reshape(tok_rows, heads_kv, group_size, HD)
    grad_four = grad_out.reshape(tok_rows, heads_kv, group_size, HD)
    query_pos = my_index * tok_rows + jnp.arange(tok_rows, dtype=jnp.int32)
    earliest = doc_start[0]

    def live_block(step_index):
        block_index = (my_index + step_index) % cycle_size
        is_live = (block_index <= my_index) & ((block_index + 1) * tok_rows > earliest)
        return (block_index, is_live)

    def forward_step(step_index, loop_carry):
        kv_keys, kv_values, stash, rowmax, row_total, acc_sum = loop_carry
        block_index, is_live = live_block(step_index)

        def forward_compute(pieces):
            old_max, old_total, old_acc = pieces
            scores = block_scores(
                query_four,
                kv_keys.reshape(tok_rows, heads_kv, HD),
                query_pos,
                doc_start,
                block_index,
                tok_rows,
                soft_scale,
            )
            new_max = jnp.maximum(old_max, jnp.max(scores, axis=-1))
            factor = jnp.exp(old_max - new_max)
            weights = jnp.exp(scores - new_max[..., None])
            new_total = old_total * factor + jnp.sum(weights, axis=-1)
            product = jnp.einsum(
                "kgqp,pkd->kgqd",
                weights.astype(jnp.bfloat16),
                kv_values.reshape(tok_rows, heads_kv, HD),
                preferred_element_type=jnp.float32,
            )
            return (new_max, new_total, old_acc * factor[..., None] + product)

        rowmax, row_total, acc_sum = lax.cond(
            is_live, forward_compute, lambda pieces: pieces, (rowmax, row_total, acc_sum)
        )
        kv_keys, kv_values = from_behind((kv_keys, kv_values), "ctx", -1)
        return (kv_keys, kv_values, stash, rowmax, row_total, acc_sum)

    start_stash = ()
    start_max = jnp.full((heads_kv, group_size, tok_rows), NEGATIVE, jnp.float32)
    start_total = jnp.zeros((heads_kv, group_size, tok_rows), jnp.float32)
    start_acc = jnp.zeros((heads_kv, group_size, tok_rows, HD), jnp.float32)
    forward_out = lax.fori_loop(
        0,
        cycle_size,
        forward_step,
        (start_keys, start_values, start_stash, start_max, start_total, start_acc),
    )
    stash, rowmax, row_total, acc_sum = (
        forward_out[2],
        forward_out[3],
        forward_out[4],
        forward_out[5],
    )
    attn_out = (acc_sum / row_total[..., None]).astype(jnp.bfloat16)
    log_total = rowmax + jnp.log(row_total)
    delta = jnp.einsum("qkgd,kgqd->kgq", grad_four, attn_out, preferred_element_type=jnp.float32)

    def backward_step(step_index, loop_carry):
        kv_keys, kv_values, grad_keys, grad_values, grad_query = loop_carry
        block_index, is_live = live_block(step_index)
        use_keys, use_values = (kv_keys, kv_values)

        def backward_compute(pieces):
            old_keys, old_values, old_query = pieces
            keys_three = use_keys.reshape(tok_rows, heads_kv, HD)
            values_three = use_values.reshape(tok_rows, heads_kv, HD)
            scores = block_scores(
                query_four, keys_three, query_pos, doc_start, block_index, tok_rows, soft_scale
            )
            probs = jnp.exp(scores - log_total[..., None])
            value_part = jnp.einsum(
                "kgqp,qkgd->pkd",
                probs.astype(jnp.bfloat16),
                grad_four,
                preferred_element_type=jnp.float32,
            )
            grad_probs = jnp.einsum(
                "qkgd,pkd->kgqp", grad_four, values_three, preferred_element_type=jnp.float32
            )
            grad_scores = (probs * (grad_probs - delta[..., None])).astype(jnp.bfloat16)
            query_part = (
                jnp.einsum(
                    "kgqp,pkd->qkgd", grad_scores, keys_three, preferred_element_type=jnp.float32
                )
                * soft_scale
            )
            key_part = (
                jnp.einsum(
                    "kgqp,qkgd->pkd", grad_scores, query_four, preferred_element_type=jnp.float32
                )
                * soft_scale
            )
            new_keys = old_keys + key_part.reshape(tok_rows, heads_kv * HD)
            new_values = old_values + value_part.reshape(tok_rows, heads_kv * HD)
            return (new_keys, new_values, old_query + query_part)

        grad_keys, grad_values, grad_query = lax.cond(
            is_live, backward_compute, lambda pieces: pieces, (grad_keys, grad_values, grad_query)
        )
        kv_keys, kv_values = from_behind((kv_keys, kv_values), "ctx", -1)
        grad_keys, grad_values = (
            from_behind(grad_keys.astype(jnp.bfloat16), "ctx", -1).astype(grad_keys.dtype),
            from_behind(grad_values.astype(jnp.bfloat16), "ctx", -1).astype(grad_values.dtype),
        )
        return (kv_keys, kv_values, grad_keys, grad_values, grad_query)

    zeros_kv = jnp.zeros((tok_rows, kv_cols), jnp.float32)
    zeros_query = jnp.zeros((tok_rows, heads_kv, group_size, HD), jnp.float32)
    backward_out = lax.fori_loop(
        0, cycle_size, backward_step, (start_keys, start_values, zeros_kv, zeros_kv, zeros_query)
    )
    grad_keys, grad_values, grad_acc = (backward_out[2], backward_out[3], backward_out[4])
    grad_query = grad_acc.reshape(tok_rows, heads_kv * group_size * HD).astype(jnp.bfloat16)
    grad_key = grad_keys.astype(jnp.bfloat16)
    grad_value = grad_values.astype(jnp.bfloat16)
    partial_input = jnp.einsum(
        "rc,dc->rd", grad_key, key_weight, preferred_element_type=jnp.float32
    )
    partial_input = partial_input + jnp.einsum(
        "rc,dc->rd", grad_value, value_weight, preferred_element_type=jnp.float32
    )
    grad_input = lax.psum_scatter(
        partial_input.astype(jnp.bfloat16), "tp", scatter_dimension=1, tiled=True
    )
    return (grad_query, grad_key, grad_value, grad_input)


def solution(mesh):
    in_specs = (
        P("ctx", "tp"),
        P("ctx", "tp"),
        P("ctx", "tp"),
        P("ctx", "tp"),
        P(None, "tp"),
        P(None, "tp"),
        P("ctx"),
    )
    out_specs = (P("ctx", "tp"), P("ctx", "tp"), P("ctx", "tp"), P("ctx", "tp"))
    return jax.shard_map(shards, mesh=mesh, in_specs=in_specs, out_specs=out_specs, check_vma=False)
```

profile of v0, /device:TPU:8, one launch (start us, length us, event | category | flops | bytes accessed | tf_op | source)
XLA Modules:
  0.0 565.8 jit_solution(7088605292721757672)
XLA Ops:
  13.3 222.7 %while.48 = (s32[]{:T(128)}, bf16[128,128]{1,0:T(8,128)(2,1)S(1)}, bf16[128,128]{1,0:T(8,128)(2,1)S(1)}, f32[1,8,128]{2,1,0:T(8,128)S(1)}, f32[1,8,128]{2,1,0:T(...) while((s32[]{:T(128)}, bf16[128,128]{1,0:T(8,128)(2,1)S(1)}, ...), condition=%wide.region_5.6_spmd.clone, body=%wide.region_0.5_spmd.clone.sunk | while | flops 68341008 | bytes 3444780 | solution.py:88
  13.9 5.2 collective-permute-start
  237.7 236.7 %while.49 = (s32[]{:T(128)}, bf16[128,128]{1,0:T(8,128)(2,1)S(1)}, bf16[128,128]{1,0:T(8,128)(2,1)S(1)}, f32[128,128]{1,0:T(8,128)S(1)}, f32[128,128]{1,0:T(8,12...) while((s32[]{:T(128)}, bf16[128,128]{1,0:T(8,128)(2,1)S(1)}, ...), condition=%wide.region_9.10_spmd.clone, body=%wide.region_6.9_spmd.clone.sunk | while | flops 169148688 | bytes 6172854 | solution.py:155
  245.7 4.1 collective-permute-start.5
  252.5 4.1 collective-permute-start.5
  259.2 4.1 collective-permute-start.5
  265.9 4.1 collective-permute-start.5
  272.6 4.1 collective-permute-start.5
  279.3 4.1 collective-permute-start.5
  286.1 4.1 collective-permute-start.5
  292.8 4.1 collective-permute-start.5
  299.5 4.1 collective-permute-start.5
  306.2 4.1 collective-permute-start.5
  312.9 4.1 collective-permute-start.5
  319.7 4.1 collective-permute-start.5
  326.4 4.1 collective-permute-start.5
  353.3 5.4 collective-permute-start.5
  361.3 5.4 collective-permute-start.5
  369.4 5.4 collective-permute-start.5
  377.5 5.4 collective-permute-start.5
  385.6 5.4 collective-permute-start.5
  393.7 5.4 collective-permute-start.5
  401.8 5.4 collective-permute-start.5
  409.9 5.4 collective-permute-start.5
  417.9 5.4 collective-permute-start.5
  426.0 5.4 collective-permute-start.5
  434.1 5.4 collective-permute-start.5
  442.2 5.4 collective-permute-start.5
  450.3 5.4 collective-permute-start.5
  458.4 5.4 collective-permute-start.5
  466.4 5.4 collective-permute-start.5
  479.1 79.9 %reduce-scatter.2.cloned.1.call-done = bf16[128,1024]{1,0:T(8,128)(2,1)} async-done(((bf16[128,8192]{1,0:T(8,128)(2,1)}), bf16[128,1024]{1,0:T(8,128)(2,1)}) %reduce-scatter.2.cloned.1.call-update) | async-done | bytes 262160 | tf_op jit(solution)/shard_map/reduce_scatter | solution.py:168
  (824 shorter events, 330.9 us)
Async XLA Ops:
  7.2 551.8 %reduce-scatter.2.cloned.1.call-start = ((), (), s32[]{:S(2)}) async-start(), calls=%async_computation.1 | async-start | bytes 2359296 | tf_op jit(solution)/shard_map/reduce_scatter | solution.py:168
  13.9 9.0 %collective-permute-start = (bf16[128,128]{1,0:T(8,128)(2,1)}, bf16[128,128]{1,0:T(8,128)(2,1)S(1)}, u32[]{:S(2)}, u32[]{:S(2)}) collective-permute-start(bf16[128,128]{1,0:T(8,128)(2,1)} %copy.54), channel_id=1, source_target_pairs={{0,248},{8,0},{16,8},{24,16},{32,24},{40,32},{48,40},{56,48},{64,5... | collective-permute-start | bytes 98312 | tf_op jit(solution)/shard_map/while/body/eval_jaxpr/ppermute | solution.py:19
  29.8 5.7 %collective-permute-start = (bf16[128,128]{1,0:T(8,128)(2,1)}, bf16[128,128]{1,0:T(8,128)(2,1)S(1)}, u32[]{:S(2)}, u32[]{:S(2)}) collective-permute-start(bf16[128,128]{1,0:T(8,128)(2,1)} %copy.54), channel_id=1, source_target_pairs={{0,248},{8,0},{16,8},{24,16},{32,24},{40,32},{48,40},{56,48},{64,5... | collective-permute-start | bytes 98312 | tf_op jit(solution)/shard_map/while/body/eval_jaxpr/ppermute | solution.py:19
  36.7 5.7 %collective-permute-start = (bf16[128,128]{1,0:T(8,128)(2,1)}, bf16[128,128]{1,0:T(8,128)(2,1)S(1)}, u32[]{:S(2)}, u32[]{:S(2)}) collective-permute-start(bf16[128,128]{1,0:T(8,128)(2,1)} %copy.54), channel_id=1, source_target_pairs={{0,248},{8,0},{16,8},{24,16},{32,24},{40,32},{48,40},{56,48},{64,5... | collective-permute-start | bytes 98312 | tf_op jit(solution)/shard_map/while/body/eval_jaxpr/ppermute | solution.py:19
  43.6 5.7 %collective-permute-start = (bf16[128,128]{1,0:T(8,128)(2,1)}, bf16[128,128]{1,0:T(8,128)(2,1)S(1)}, u32[]{:S(2)}, u32[]{:S(2)}) collective-permute-start(bf16[128,128]{1,0:T(8,128)(2,1)} %copy.54), channel_id=1, source_target_pairs={{0,248},{8,0},{16,8},{24,16},{32,24},{40,32},{48,40},{56,48},{64,5... | collective-permute-start | bytes 98312 | tf_op jit(solution)/shard_map/while/body/eval_jaxpr/ppermute | solution.py:19
  50.5 5.7 %collective-permute-start = (bf16[128,128]{1,0:T(8,128)(2,1)}, bf16[128,128]{1,0:T(8,128)(2,1)S(1)}, u32[]{:S(2)}, u32[]{:S(2)}) collective-permute-start(bf16[128,128]{1,0:T(8,128)(2,1)} %copy.54), channel_id=1, source_target_pairs={{0,248},{8,0},{16,8},{24,16},{32,24},{40,32},{48,40},{56,48},{64,5... | collective-permute-start | bytes 98312 | tf_op jit(solution)/shard_map/while/body/eval_jaxpr/ppermute | solution.py:19
  57.4 5.7 %collective-permute-start = (bf16[128,128]{1,0:T(8,128)(2,1)}, bf16[128,128]{1,0:T(8,128)(2,1)S(1)}, u32[]{:S(2)}, u32[]{:S(2)}) collective-permute-start(bf16[128,128]{1,0:T(8,128)(2,1)} %copy.54), channel_id=1, source_target_pairs={{0,248},{8,0},{16,8},{24,16},{32,24},{40,32},{48,40},{56,48},{64,5... | collective-permute-start | bytes 98312 | tf_op jit(solution)/shard_map/while/body/eval_jaxpr/ppermute | solution.py:19
  64.3 5.7 %collective-permute-start = (bf16[128,128]{1,0:T(8,128)(2,1)}, bf16[128,128]{1,0:T(8,128)(2,1)S(1)}, u32[]{:S(2)}, u32[]{:S(2)}) collective-permute-start(bf16[128,128]{1,0:T(8,128)(2,1)} %copy.54), channel_id=1, source_target_pairs={{0,248},{8,0},{16,8},{24,16},{32,24},{40,32},{48,40},{56,48},{64,5... | collective-permute-start | bytes 98312 | tf_op jit(solution)/shard_map/while/body/eval_jaxpr/ppermute | solution.py:19
  71.2 5.7 %collective-permute-start = (bf16[128,128]{1,0:T(8,128)(2,1)}, bf16[128,128]{1,0:T(8,128)(2,1)S(1)}, u32[]{:S(2)}, u32[]{:S(2)}) collective-permute-start(bf16[128,128]{1,0:T(8,128)(2,1)} %copy.54), channel_id=1, source_target_pairs={{0,248},{8,0},{16,8},{24,16},{32,24},{40,32},{48,40},{56,48},{64,5... | collective-permute-start | bytes 98312 | tf_op jit(solution)/shard_map/while/body/eval_jaxpr/ppermute | solution.py:19
  85.0 5.7 %collective-permute-start = (bf16[128,128]{1,0:T(8,128)(2,1)}, bf16[128,128]{1,0:T(8,128)(2,1)S(1)}, u32[]{:S(2)}, u32[]{:S(2)}) collective-permute-start(bf16[128,128]{1,0:T(8,128)(2,1)} %copy.54), channel_id=1, source_target_pairs={{0,248},{8,0},{16,8},{24,16},{32,24},{40,32},{48,40},{56,48},{64,5... | collective-permute-start | bytes 98312 | tf_op jit(solution)/shard_map/while/body/eval_jaxpr/ppermute | solution.py:19
  98.8 5.7 %collective-permute-start = (bf16[128,128]{1,0:T(8,128)(2,1)}, bf16[128,128]{1,0:T(8,128)(2,1)S(1)}, u32[]{:S(2)}, u32[]{:S(2)}) collective-permute-start(bf16[128,128]{1,0:T(8,128)(2,1)} %copy.54), channel_id=1, source_target_pairs={{0,248},{8,0},{16,8},{24,16},{32,24},{40,32},{48,40},{56,48},{64,5... | collective-permute-start | bytes 98312 | tf_op jit(solution)/shard_map/while/body/eval_jaxpr/ppermute | solution.py:19
  112.6 5.7 %collective-permute-start = (bf16[128,128]{1,0:T(8,128)(2,1)}, bf16[128,128]{1,0:T(8,128)(2,1)S(1)}, u32[]{:S(2)}, u32[]{:S(2)}) collective-permute-start(bf16[128,128]{1,0:T(8,128)(2,1)} %copy.54), channel_id=1, source_target_pairs={{0,248},{8,0},{16,8},{24,16},{32,24},{40,32},{48,40},{56,48},{64,5... | collective-permute-start | bytes 98312 | tf_op jit(solution)/shard_map/while/body/eval_jaxpr/ppermute | solution.py:19
  126.4 5.7 %collective-permute-start = (bf16[128,128]{1,0:T(8,128)(2,1)}, bf16[128,128]{1,0:T(8,128)(2,1)S(1)}, u32[]{:S(2)}, u32[]{:S(2)}) collective-permute-start(bf16[128,128]{1,0:T(8,128)(2,1)} %copy.54), channel_id=1, source_target_pairs={{0,248},{8,0},{16,8},{24,16},{32,24},{40,32},{48,40},{56,48},{64,5... | collective-permute-start | bytes 98312 | tf_op jit(solution)/shard_map/while/body/eval_jaxpr/ppermute | solution.py:19
  140.1 5.7 %collective-permute-start = (bf16[128,128]{1,0:T(8,128)(2,1)}, bf16[128,128]{1,0:T(8,128)(2,1)S(1)}, u32[]{:S(2)}, u32[]{:S(2)}) collective-permute-start(bf16[128,128]{1,0:T(8,128)(2,1)} %copy.54), channel_id=1, source_target_pairs={{0,248},{8,0},{16,8},{24,16},{32,24},{40,32},{48,40},{56,48},{64,5... | collective-permute-start | bytes 98312 | tf_op jit(solution)/shard_map/while/body/eval_jaxpr/ppermute | solution.py:19
  153.9 5.7 %collective-permute-start = (bf16[128,128]{1,0:T(8,128)(2,1)}, bf16[128,128]{1,0:T(8,128)(2,1)S(1)}, u32[]{:S(2)}, u32[]{:S(2)}) collective-permute-start(bf16[128,128]{1,0:T(8,128)(2,1)} %copy.54), channel_id=1, source_target_pairs={{0,248},{8,0},{16,8},{24,16},{32,24},{40,32},{48,40},{56,48},{64,5... | collective-permute-start | bytes 98312 | tf_op jit(solution)/shard_map/while/body/eval_jaxpr/ppermute | solution.py:19
  216.0 5.7 %collective-permute-start = (bf16[128,128]{1,0:T(8,128)(2,1)}, bf16[128,128]{1,0:T(8,128)(2,1)S(1)}, u32[]{:S(2)}, u32[]{:S(2)}) collective-permute-start(bf16[128,128]{1,0:T(8,128)(2,1)} %copy.54), channel_id=1, source_target_pairs={{0,248},{8,0},{16,8},{24,16},{32,24},{40,32},{48,40},{56,48},{64,5... | collective-permute-start | bytes 98312 | tf_op jit(solution)/shard_map/while/body/eval_jaxpr/ppermute | solution.py:19
  229.8 5.7 %collective-permute-start = (bf16[128,128]{1,0:T(8,128)(2,1)}, bf16[128,128]{1,0:T(8,128)(2,1)S(1)}, u32[]{:S(2)}, u32[]{:S(2)}) collective-permute-start(bf16[128,128]{1,0:T(8,128)(2,1)} %copy.54), channel_id=1, source_target_pairs={{0,248},{8,0},{16,8},{24,16},{32,24},{40,32},{48,40},{56,48},{64,5... | collective-permute-start | bytes 98312 | tf_op jit(solution)/shard_map/while/body/eval_jaxpr/ppermute | solution.py:19
  353.3 7.0 %collective-permute-start.5 = (bf16[128,128]{1,0:T(8,128)(2,1)S(1)}, bf16[128,128]{1,0:T(8,128)(2,1)S(1)}, u32[]{:S(2)}, u32[]{:S(2)}) collective-permute-start(bf16[128,128]{1,0:T(8,128)(2,1)S(1)} %convert_element_type.124), channel_id=1, source_target_pairs={{0,248},{8,0},{16,8},{24,16},{32,24},{40,32},{48,40},{56,48},{64,5... | collective-permute-start | bytes 98312 | tf_op jit(solution)/shard_map/while/body/eval_jaxpr/ppermute | solution.py:19
  361.3 7.0 %collective-permute-start.5 = (bf16[128,128]{1,0:T(8,128)(2,1)S(1)}, bf16[128,128]{1,0:T(8,128)(2,1)S(1)}, u32[]{:S(2)}, u32[]{:S(2)}) collective-permute-start(bf16[128,128]{1,0:T(8,128)(2,1)S(1)} %convert_element_type.124), channel_id=1, source_target_pairs={{0,248},{8,0},{16,8},{24,16},{32,24},{40,32},{48,40},{56,48},{64,5... | collective-permute-start | bytes 98312 | tf_op jit(solution)/shard_map/while/body/eval_jaxpr/ppermute | solution.py:19
  369.4 7.0 %collective-permute-start.5 = (bf16[128,128]{1,0:T(8,128)(2,1)S(1)}, bf16[128,128]{1,0:T(8,128)(2,1)S(1)}, u32[]{:S(2)}, u32[]{:S(2)}) collective-permute-start(bf16[128,128]{1,0:T(8,128)(2,1)S(1)} %convert_element_type.124), channel_id=1, source_target_pairs={{0,248},{8,0},{16,8},{24,16},{32,24},{40,32},{48,40},{56,48},{64,5... | collective-permute-start | bytes 98312 | tf_op jit(solution)/shard_map/while/body/eval_jaxpr/ppermute | solution.py:19
  377.5 7.0 %collective-permute-start.5 = (bf16[128,128]{1,0:T(8,128)(2,1)S(1)}, bf16[128,128]{1,0:T(8,128)(2,1)S(1)}, u32[]{:S(2)}, u32[]{:S(2)}) collective-permute-start(bf16[128,128]{1,0:T(8,128)(2,1)S(1)} %convert_element_type.124), channel_id=1, source_target_pairs={{0,248},{8,0},{16,8},{24,16},{32,24},{40,32},{48,40},{56,48},{64,5... | collective-permute-start | bytes 98312 | tf_op jit(solution)/shard_map/while/body/eval_jaxpr/ppermute | solution.py:19
  385.6 7.0 %collective-permute-start.5 = (bf16[128,128]{1,0:T(8,128)(2,1)S(1)}, bf16[128,128]{1,0:T(8,128)(2,1)S(1)}, u32[]{:S(2)}, u32[]{:S(2)}) collective-permute-start(bf16[128,128]{1,0:T(8,128)(2,1)S(1)} %convert_element_type.124), channel_id=1, source_target_pairs={{0,248},{8,0},{16,8},{24,16},{32,24},{40,32},{48,40},{56,48},{64,5... | collective-permute-start | bytes 98312 | tf_op jit(solution)/shard_map/while/body/eval_jaxpr/ppermute | solution.py:19
  393.7 7.0 %collective-permute-start.5 = (bf16[128,128]{1,0:T(8,128)(2,1)S(1)}, bf16[128,128]{1,0:T(8,128)(2,1)S(1)}, u32[]{:S(2)}, u32[]{:S(2)}) collective-permute-start(bf16[128,128]{1,0:T(8,128)(2,1)S(1)} %convert_element_type.124), channel_id=1, source_target_pairs={{0,248},{8,0},{16,8},{24,16},{32,24},{40,32},{48,40},{56,48},{64,5... | collective-permute-start | bytes 98312 | tf_op jit(solution)/shard_map/while/body/eval_jaxpr/ppermute | solution.py:19
  401.8 7.0 %collective-permute-start.5 = (bf16[128,128]{1,0:T(8,128)(2,1)S(1)}, bf16[128,128]{1,0:T(8,128)(2,1)S(1)}, u32[]{:S(2)}, u32[]{:S(2)}) collective-permute-start(bf16[128,128]{1,0:T(8,128)(2,1)S(1)} %convert_element_type.124), channel_id=1, source_target_pairs={{0,248},{8,0},{16,8},{24,16},{32,24},{40,32},{48,40},{56,48},{64,5... | collective-permute-start | bytes 98312 | tf_op jit(solution)/shard_map/while/body/eval_jaxpr/ppermute | solution.py:19
  409.9 7.0 %collective-permute-start.5 = (bf16[128,128]{1,0:T(8,128)(2,1)S(1)}, bf16[128,128]{1,0:T(8,128)(2,1)S(1)}, u32[]{:S(2)}, u32[]{:S(2)}) collective-permute-start(bf16[128,128]{1,0:T(8,128)(2,1)S(1)} %convert_element_type.124), channel_id=1, source_target_pairs={{0,248},{8,0},{16,8},{24,16},{32,24},{40,32},{48,40},{56,48},{64,5... | collective-permute-start | bytes 98312 | tf_op jit(solution)/shard_map/while/body/eval_jaxpr/ppermute | solution.py:19
  417.9 7.0 %collective-permute-start.5 = (bf16[128,128]{1,0:T(8,128)(2,1)S(1)}, bf16[128,128]{1,0:T(8,128)(2,1)S(1)}, u32[]{:S(2)}, u32[]{:S(2)}) collective-permute-start(bf16[128,128]{1,0:T(8,128)(2,1)S(1)} %convert_element_type.124), channel_id=1, source_target_pairs={{0,248},{8,0},{16,8},{24,16},{32,24},{40,32},{48,40},{56,48},{64,5... | collective-permute-start | bytes 98312 | tf_op jit(solution)/shard_map/while/body/eval_jaxpr/ppermute | solution.py:19
  426.0 7.0 %collective-permute-start.5 = (bf16[128,128]{1,0:T(8,128)(2,1)S(1)}, bf16[128,128]{1,0:T(8,128)(2,1)S(1)}, u32[]{:S(2)}, u32[]{:S(2)}) collective-permute-start(bf16[128,128]{1,0:T(8,128)(2,1)S(1)} %convert_element_type.124), channel_id=1, source_target_pairs={{0,248},{8,0},{16,8},{24,16},{32,24},{40,32},{48,40},{56,48},{64,5... | collective-permute-start | bytes 98312 | tf_op jit(solution)/shard_map/while/body/eval_jaxpr/ppermute | solution.py:19
  434.1 7.0 %collective-permute-start.5 = (bf16[128,128]{1,0:T(8,128)(2,1)S(1)}, bf16[128,128]{1,0:T(8,128)(2,1)S(1)}, u32[]{:S(2)}, u32[]{:S(2)}) collective-permute-start(bf16[128,128]{1,0:T(8,128)(2,1)S(1)} %convert_element_type.124), channel_id=1, source_target_pairs={{0,248},{8,0},{16,8},{24,16},{32,24},{40,32},{48,40},{56,48},{64,5... | collective-permute-start | bytes 98312 | tf_op jit(solution)/shard_map/while/body/eval_jaxpr/ppermute | solution.py:19
  442.2 7.0 %collective-permute-start.5 = (bf16[128,128]{1,0:T(8,128)(2,1)S(1)}, bf16[128,128]{1,0:T(8,128)(2,1)S(1)}, u32[]{:S(2)}, u32[]{:S(2)}) collective-permute-start(bf16[128,128]{1,0:T(8,128)(2,1)S(1)} %convert_element_type.124), channel_id=1, source_target_pairs={{0,248},{8,0},{16,8},{24,16},{32,24},{40,32},{48,40},{56,48},{64,5... | collective-permute-start | bytes 98312 | tf_op jit(solution)/shard_map/while/body/eval_jaxpr/ppermute | solution.py:19
  450.3 7.0 %collective-permute-start.5 = (bf16[128,128]{1,0:T(8,128)(2,1)S(1)}, bf16[128,128]{1,0:T(8,128)(2,1)S(1)}, u32[]{:S(2)}, u32[]{:S(2)}) collective-permute-start(bf16[128,128]{1,0:T(8,128)(2,1)S(1)} %convert_element_type.124), channel_id=1, source_target_pairs={{0,248},{8,0},{16,8},{24,16},{32,24},{40,32},{48,40},{56,48},{64,5... | collective-permute-start | bytes 98312 | tf_op jit(solution)/shard_map/while/body/eval_jaxpr/ppermute | solution.py:19
  458.4 7.0 %collective-permute-start.5 = (bf16[128,128]{1,0:T(8,128)(2,1)S(1)}, bf16[128,128]{1,0:T(8,128)(2,1)S(1)}, u32[]{:S(2)}, u32[]{:S(2)}) collective-permute-start(bf16[128,128]{1,0:T(8,128)(2,1)S(1)} %convert_element_type.124), channel_id=1, source_target_pairs={{0,248},{8,0},{16,8},{24,16},{32,24},{40,32},{48,40},{56,48},{64,5... | collective-permute-start | bytes 98312 | tf_op jit(solution)/shard_map/while/body/eval_jaxpr/ppermute | solution.py:19
  466.4 7.0 %collective-permute-start.5 = (bf16[128,128]{1,0:T(8,128)(2,1)S(1)}, bf16[128,128]{1,0:T(8,128)(2,1)S(1)}, u32[]{:S(2)}, u32[]{:S(2)}) collective-permute-start(bf16[128,128]{1,0:T(8,128)(2,1)S(1)} %convert_element_type.124), channel_id=1, source_target_pairs={{0,248},{8,0},{16,8},{24,16},{32,24},{40,32},{48,40},{56,48},{64,5... | collective-permute-start | bytes 98312 | tf_op jit(solution)/shard_map/while/body/eval_jaxpr/ppermute | solution.py:19
  (166 other events, 927.7 us)
Sparse Core Ops, SparseCore 0:
  478.2 80.6 reduce-scatter.1
where the time goes:
time: 569 us; the launch traced here: 566 us
  starting transfers between devices  280 us (49%)
  waiting for transfers between devices  208 us (37%)
  local copies, waits for them, and re-layouts  47.7 us (8%)
  between operations  14.2 us (2%)
  loops' own time  6.42 us (1%)
  matrix products  6.16 us (1%)
    ppermute x192, starting transfers between devices, from_behind(): return lax.ppermute(value, axis, pairs)  280 us
    ppermute x192, waiting for transfers between devices, from_behind(): return lax.ppermute(value, axis, pairs)  128 us
    reduce_scatter x1, waiting for transfers between devices, shards(): lax.psum_scatter(partial_input.astype(jnp.bfloat16), 'tp', scatter_dimens...  79.9 us
    while x128, local copies, waits for them, and re-layouts  39.6 us
  transfers between devices with their start and end apart: 193, of which 191 were waited for; matrix products, arithmetic and copies ran while one was open for 4% of the time, Pallas kernels for 0%

commit v1 on v0

v1 whole, which is shorter than its diff:
```python
import math

import jax
import jax.numpy as jnp
from jax import lax
from jax.sharding import PartitionSpec as P

HEADS = 64
KV_HEADS = 8
HD = 128
REACH = 16


NEGATIVE = -1e30


def shifted(value, axis, steps):
    count = lax.axis_size(axis)
    pairs = [(source, source + steps) for source in range(count) if 0 <= source + steps < count]
    return lax.ppermute(value, axis, pairs)


def shards(queries, key_proj, value_proj, grad_out, key_weight, value_weight, doc_start):
    tok_rows = queries.shape[0]
    heads_kv = key_proj.shape[1] // HD
    kv_cols = key_proj.shape[1]
    group_size = HEADS // KV_HEADS
    soft_scale = 1.0 / math.sqrt(HD)
    my_index = lax.axis_index("ctx")
    blocks = REACH + 1
    window = blocks * tok_rows

    own_kv = jnp.concatenate([key_proj, value_proj], axis=1)
    half = REACH // 2
    same_core = [shifted(own_kv, "ctx", 2 * (i + 1)) for i in range(half)]
    stack = jnp.concatenate([own_kv] + same_core, axis=0)
    parity = my_index % 2
    sibling = [(source, source ^ 1) for source in range(lax.axis_size("ctx"))]
    outgoing = lax.dynamic_slice_in_dim(stack, parity * tok_rows, half * tok_rows, 0)
    other_core = lax.ppermute(outgoing, "ctx", sibling)
    window_kv = jnp.concatenate([stack[tok_rows:], other_core, own_kv], axis=0)
    offsets = [2 * (i + 1) for i in range(half)] + [2 * i + 1 for i in range(half)] + [0]
    keys_three = window_kv[:, :kv_cols].reshape(window, heads_kv, HD)
    values_three = window_kv[:, kv_cols:].reshape(window, heads_kv, HD)

    query_four = queries.reshape(tok_rows, heads_kv, group_size, HD)
    grad_four = grad_out.reshape(tok_rows, heads_kv, group_size, HD)
    query_pos = my_index * tok_rows + jnp.arange(tok_rows, dtype=jnp.int32)
    block_pos = jnp.concatenate(
        [jnp.full((tok_rows,), offset, jnp.int32) for offset in offsets]
    )
    key_pos = (my_index * tok_rows - block_pos * tok_rows) + jnp.tile(
        jnp.arange(tok_rows, dtype=jnp.int32), blocks
    )
    visible = (key_pos[None, :] <= query_pos[:, None]) & (key_pos[None, :] >= doc_start[:, None])

    scores = (
        jnp.einsum("qkgd,pkd->kgqp", query_four, keys_three, preferred_element_type=jnp.float32)
        * soft_scale
    )
    scores = jnp.where(visible, scores, NEGATIVE)
    rowmax = jnp.max(scores, axis=-1)
    expw = jnp.exp(scores - rowmax[..., None])
    row_total = jnp.sum(expw, axis=-1)
    acc_sum = jnp.einsum(
        "kgqp,pkd->kgqd",
        expw.astype(jnp.bfloat16),
        values_three,
        preferred_element_type=jnp.float32,
    )
    attn_out = (acc_sum / row_total[..., None]).astype(jnp.bfloat16)
    log_total = rowmax + jnp.log(row_total)
    delta = jnp.einsum("qkgd,kgqd->kgq", grad_four, attn_out, preferred_element_type=jnp.float32)

    probs = jnp.exp(scores - log_total[..., None])
    value_part = jnp.einsum(
        "kgqp,qkgd->pkd", probs.astype(jnp.bfloat16), grad_four, preferred_element_type=jnp.float32
    )
    grad_probs = jnp.einsum(
        "qkgd,pkd->kgqp", grad_four, values_three, preferred_element_type=jnp.float32
    )
    grad_scores = (probs * (grad_probs - delta[..., None])).astype(jnp.bfloat16)
    query_part = (
        jnp.einsum("kgqp,pkd->qkgd", grad_scores, keys_three, preferred_element_type=jnp.float32)
        * soft_scale
    )
    key_part = (
        jnp.einsum("kgqp,qkgd->pkd", grad_scores, query_four, preferred_element_type=jnp.float32)
        * soft_scale
    )
    grad_query = query_part.reshape(tok_rows, heads_kv * group_size * HD).astype(jnp.bfloat16)

    partial_kv = jnp.concatenate(
        [key_part.reshape(window, kv_cols), value_part.reshape(window, kv_cols)], axis=1
    )
    span = half * tok_rows
    from_other = lax.ppermute(partial_kv[span : 2 * span].astype(jnp.bfloat16), "ctx", sibling)
    back_stack = jnp.concatenate([partial_kv[2 * span :], partial_kv[:span]], axis=0)
    back_stack = lax.dynamic_update_slice_in_dim(
        back_stack,
        lax.dynamic_slice_in_dim(back_stack, parity * tok_rows, span, 0)
        + from_other.astype(jnp.float32),
        parity * tok_rows,
        0,
    )
    total_kv = back_stack[:tok_rows]
    for i in range(half):
        piece = back_stack[(i + 1) * tok_rows : (i + 2) * tok_rows].astype(jnp.bfloat16)
        total_kv = total_kv + shifted(piece, "ctx", -2 * (i + 1)).astype(jnp.float32)
    grad_key = total_kv[:, :kv_cols].astype(jnp.bfloat16)
    grad_value = total_kv[:, kv_cols:].astype(jnp.bfloat16)

    partial_input = jnp.einsum(
        "rc,dc->rd", grad_key, key_weight, preferred_element_type=jnp.float32
    )
    partial_input = partial_input + jnp.einsum(
        "rc,dc->rd", grad_value, value_weight, preferred_element_type=jnp.float32
    )
    tp_size = lax.axis_size("tp")
    tp_index = lax.axis_index("tp")
    chunks = partial_input.astype(jnp.bfloat16).reshape(tok_rows, tp_size, -1)
    total_input = jnp.take(chunks, tp_index, axis=1).astype(jnp.float32)
    for k in range(1, tp_size):
        piece = jnp.take(chunks, (tp_index + k) % tp_size, axis=1)
        pairs = [(source, (source + k) % tp_size) for source in range(tp_size)]
        total_input = total_input + lax.ppermute(piece, "tp", pairs).astype(jnp.float32)
    grad_input = total_input.astype(jnp.bfloat16)
    return (grad_query, grad_key, grad_value, grad_input)


def solution(mesh):
    in_specs = (
        P("ctx", "tp"),
        P("ctx", "tp"),
        P("ctx", "tp"),
        P("ctx", "tp"),
        P(None, "tp"),
        P(None, "tp"),
        P("ctx"),
    )
    out_specs = (P("ctx", "tp"), P("ctx", "tp"), P("ctx", "tp"), P("ctx", "tp"))
    return jax.shard_map(shards, mesh=mesh, in_specs=in_specs, out_specs=out_specs, check_vma=False)
```

time: 569 us -> 138 us (0.24)
  starting transfers between devices: 280 us -> 60.8 us
  waiting for transfers between devices: 208 us -> 25.6 us
  local copies, waits for them, and re-layouts: 47.7 us -> 25.1 us
  between operations: 14.2 us -> 1.39 us
  matrix products: 6.16 us -> 14 us
  other arithmetic: 3.11 us -> 10.4 us
  loops' own time: 6.42 us -> 0 us
    ppermute x192 -> x25, starting transfers between devices: 280 us -> 60.8 us  [the longest x16 44 us: shifted(): return lax.ppermute(value, axis, pairs)]
    ppermute x192 -> x25, waiting for transfers between devices: 128 us -> 25.6 us  [the longest x7 12.6 us: shards(): lax.ppermute(piece, 'tp', pairs).astype(jnp.float32)]
    reduce_scatter x1 -> x0, waiting for transfers between devices: 79.9 us -> none  [shards(): lax.psum_scatter(partial_input.astype(jnp.bfloat16), 'tp', scatter_dimens...]
    while x128 -> x0, local copies, waits for them, and re-layouts: 39.6 us -> none
    unnamed x20 -> x58, local copies, waits for them, and re-layouts: 7.61 us -> 17.6 us
    dot_general x7 -> x6, matrix products: 3.41 us -> 12.6 us  [the longest x1 5.31 us: shards(): jnp.einsum('kgqp,qkgd->pkd', probs.astype(jnp.bfloat16), grad_four, prefe...]
    another operation x66 -> x0, loops' own time: 6.42 us -> none  [the longest x1 3.16 us: shards(): lax.fori_loop(0, cycle_size, backward_step, (start_keys, start_values, ze...]
  transfers between devices with their start and end apart: 193 -> 25, of which waited for: 191 -> 13; matrix products, arithmetic and copies ran while one was open for 4% -> 10% of each run, Pallas kernels for 0% -> 0%
where the time goes in v1:
time: 138 us; the launch traced here: 137 us
  starting transfers between devices  60.8 us (44%)
  waiting for transfers between devices  25.6 us (19%)
  local copies, waits for them, and re-layouts  25.1 us (18%)
  matrix products  14 us (10%)
  other arithmetic  10.4 us (8%)
  between operations  1.39 us (1%)
    ppermute x16, starting transfers between devices, shifted(): return lax.ppermute(value, axis, pairs)  44 us
    unnamed x58, local copies, waits for them, and re-layouts  17.6 us
    ppermute x7, starting transfers between devices, shards(): lax.ppermute(piece, 'tp', pairs).astype(jnp.float32)  16.4 us
    ppermute x7, waiting for transfers between devices, shards(): lax.ppermute(piece, 'tp', pairs).astype(jnp.float32)  12.6 us
    ppermute x16, waiting for transfers between devices, shifted(): return lax.ppermute(value, axis, pairs)  10.5 us
    dot_general x1, matrix products, shards(): jnp.einsum('kgqp,qkgd->pkd', probs.astype(jnp.bfloat16), grad_four, prefe...  5.31 us
    another operation x1, local copies, waits for them, and re-layouts, shards(): total_input = jnp.take(chunks, tp_index, axis=1).astype(jnp.float32)  4.6 us
    select_n x7, other arithmetic, shards(): piece = jnp.take(chunks, (tp_index + k) % tp_size, axis=1)  3.56 us
  transfers between devices with their start and end apart: 25, of which 13 were waited for; matrix products, arithmetic and copies ran while one was open for 10% of the time, Pallas kernels for 0%

profile of v1, /device:TPU:8, one launch (start us, length us, event | category | flops | bytes accessed | tf_op | source)
XLA Modules:
  0.0 137.2 jit_solution(8576482134517946218)
XLA Ops:
  0.7 1.5 %constant_dynamic-update-slice_fusion.11 = (bf16[1152,256]{1,0:T(8,128)(2,1)}, bf16[128,256]{1,0:T(8,128)(2,1)S(1)}) fusion(bf16[128,128]{1,0:T(8,128)(2,1)} %param.10), kind=kLoop, calls=%fused_computation.81 | loop fusion | bytes 98304
  3.6 3.8 %collective-permute-start = (bf16[128,256]{1,0:T(8,128)(2,1)S(1)}, bf16[128,256]{1,0:T(8,128)(2,1)S(1)}, u32[]{:S(2)}, u32[]{:S(2)}) collective-permute-start(bf16[128,256]{1,0:T(8,128)(2,1)S(1)} %get-tuple-element.55), channel_id=1, source_target_pairs={{0,16},{8,24},{16,32},{24,40},{32,48},{40,56},{48,64},{56,72},{64,... | collective-permute-start | bytes 196616 | tf_op jit(solution)/shard_map/ppermute | solution.py:20
  7.4 5.2 %collective-permute-start.1 = (bf16[128,256]{1,0:T(8,128)(2,1)S(1)}, bf16[128,256]{1,0:T(8,128)(2,1)S(1)}, u32[]{:S(2)}, u32[]{:S(2)}) collective-permute-start(bf16[128,256]{1,0:T(8,128)(2,1)S(1)} %get-tuple-element.55), channel_id=1, source_target_pairs={{0,32},{8,40},{16,48},{24,56},{32,64},{40,72},{48,80},{56,88},{64,... | collective-permute-start | bytes 196616 | tf_op jit(solution)/shard_map/ppermute | solution.py:20
  12.6 5.9 %collective-permute-start.2 = (bf16[128,256]{1,0:T(8,128)(2,1)S(1)}, bf16[128,256]{1,0:T(8,128)(2,1)S(1)}, u32[]{:S(2)}, u32[]{:S(2)}) collective-permute-start(bf16[128,256]{1,0:T(8,128)(2,1)S(1)} %get-tuple-element.55), channel_id=1, source_target_pairs={{0,48},{8,56},{16,64},{24,72},{32,80},{40,88},{48,96},{56,104},{64... | collective-permute-start | bytes 196616 | tf_op jit(solution)/shard_map/ppermute | solution.py:20
  18.6 2.4 %collective-permute-start.3 = (bf16[128,256]{1,0:T(8,128)(2,1)S(1)}, bf16[128,256]{1,0:T(8,128)(2,1)S(1)}, u32[]{:S(2)}, u32[]{:S(2)}) collective-permute-start(bf16[128,256]{1,0:T(8,128)(2,1)S(1)} %get-tuple-element.55), channel_id=1, source_target_pairs={{0,64},{8,72},{16,80},{24,88},{32,96},{40,104},{48,112},{56,120},{... | collective-permute-start | bytes 196616 | tf_op jit(solution)/shard_map/ppermute | solution.py:20
  20.9 1.9 %collective-permute-start.4 = (bf16[128,256]{1,0:T(8,128)(2,1)S(1)}, bf16[128,256]{1,0:T(8,128)(2,1)S(1)}, u32[]{:S(2)}, u32[]{:S(2)}) collective-permute-start(bf16[128,256]{1,0:T(8,128)(2,1)S(1)} %get-tuple-element.55), channel_id=1, source_target_pairs={{0,80},{8,88},{16,96},{24,104},{32,112},{40,120},{48,128},{56,136}... | collective-permute-start | bytes 196616 | tf_op jit(solution)/shard_map/ppermute | solution.py:20
  24.4 1.9 %collective-permute-start.5 = (bf16[128,256]{1,0:T(8,128)(2,1)S(1)}, bf16[128,256]{1,0:T(8,128)(2,1)S(1)}, u32[]{:S(2)}, u32[]{:S(2)}) collective-permute-start(bf16[128,256]{1,0:T(8,128)(2,1)S(1)} %get-tuple-element.55), channel_id=1, source_target_pairs={{0,96},{8,104},{16,112},{24,120},{32,128},{40,136},{48,144},{56,15... | collective-permute-start | bytes 196616 | tf_op jit(solution)/shard_map/ppermute | solution.py:20
  26.9 1.9 %collective-permute-start.6 = (bf16[128,256]{1,0:T(8,128)(2,1)S(1)}, bf16[128,256]{1,0:T(8,128)(2,1)S(1)}, u32[]{:S(2)}, u32[]{:S(2)}) collective-permute-start(bf16[128,256]{1,0:T(8,128)(2,1)S(1)} %get-tuple-element.55), channel_id=1, source_target_pairs={{0,112},{8,120},{16,128},{24,136},{32,144},{40,152},{48,160},{56,1... | collective-permute-start | bytes 196616 | tf_op jit(solution)/shard_map/ppermute | solution.py:20
  34.2 2.2 %collective-permute-done.5 = bf16[128,256]{1,0:T(8,128)(2,1)S(1)} collective-permute-done((bf16[128,256]{1,0:T(8,128)(2,1)S(1)}, bf16[128,256]{1,0:T(8,128)(2,1)S(1)}, u32[]{:S(2)}, u32[]{:S(2)}) %collective-permute-start.5) | collective-permute-done | bytes 65568 | tf_op jit(solution)/shard_map/ppermute | solution.py:20
  44.9 2.3 %copy-done.1 = f32[1,8,128,2176]{2,3,1,0:T(8,128)} copy-done((f32[1,8,128,2176]{2,3,1,0:T(8,128)}, f32[1,8,128,2176]{2,3,1,0:T(8,128)S(1)}, u32[]{:S(2)}) %copy-start.1) | copy-done | bytes 8912920
  49.1 5.3 %fusion.15 = f32[2176,128]{0,1:T(8,128)S(1)} fusion(bf16[128,8,128]{0,2,1:T(8,128)(2,1)S(1)} %copy.18, f32[1,8,128,2176]{2,3,1,0:T(8,128)} %copy-done.1, f32[8,128]{1,0:T(8,128)S(1)} %log_add_fusion), kind=kOutput, calls=%fused_computation.18 | convolution fusion | flops 574881792 | bytes 10293248 | tf_op jit(solution)/shard_map/kgqp,qkgd->pkd/dot_general | solution.py:76
  55.5 2.0 %fusion.6 = bf16[8,128,2176]{1,2,0:T(8,128)(2,1)S(1)} fusion(bf16[128,8,128]{0,2,1:T(8,128)(2,1)S(1)} %copy.18, f32[1,8,128,2176]{2,3,1,0:T(8,128)S(1)} %bitcast.88, f32[8,128]{1,0:T(8,128)S(1)} %copy.35, f32[8,128]{1,0:T(8,128)S(1)} %log_add_fusion, bf16[2176,256]{1,0:T(8,128)(2,1)S(1)} %copy-done.4), kind=kOutput, calls=%fused_computation.11 | convolution fusion | flops 579338240 | bytes 14196736 | tf_op jit(solution)/shard_map/qkgd,pkd->kgqp/dot_general | solution.py:79
  57.6 1.5 %fusion.18 = f32[2176,128]{0,1:T(8,128)S(1)} fusion(bf16[8,128,2176]{1,2,0:T(8,128)(2,1)S(1)} %fusion.6, bf16[128,8,128]{0,2,1:T(8,128)(2,1)S(1)} %bitcast.94), kind=kOutput, calls=%fused_computation.20 | convolution fusion | flops 570703872 | bytes 5832704 | tf_op jit(solution)/shard_map/kgqp,qkgd->pkd/dot_general | solution.py:88
  60.2 1.5 %collective-permute-done.9 = bf16[1024,256]{0,1:T(8,128)(2,1)S(1)} collective-permute-done((bf16[1024,256]{0,1:T(8,128)(2,1)S(1)}, bf16[1024,256]{0,1:T(8,128)(2,1)S(1)}, u32[]{:S(2)}, u32[]{:S(2)}) %collective-permute-start.9) | collective-permute-done | bytes 524320 | tf_op jit(solution)/shard_map/ppermute | solution.py:97
  62.6 3.3 %collective-permute-start.17 = (bf16[128,256]{0,1:T(8,128)(2,1)S(1)}, bf16[128,256]{0,1:T(8,128)(2,1)}, u32[]{:S(2)}, u32[]{:S(2)}) collective-permute-start(bf16[128,256]{0,1:T(8,128)(2,1)S(1)} %get-tuple-element.29), channel_id=1, source_target_pairs={{128,0},{136,8},{144,16},{152,24},{160,32},{168,40},{176,48},{184,... | collective-permute-start | bytes 196616 | tf_op jit(solution)/shard_map/ppermute | solution.py:20
  65.9 1.9 %collective-permute-start.16 = (bf16[128,256]{0,1:T(8,128)(2,1)S(1)}, bf16[128,256]{0,1:T(8,128)(2,1)S(1)}, u32[]{:S(2)}, u32[]{:S(2)}) collective-permute-start(bf16[128,256]{0,1:T(8,128)(2,1)S(1)} %get-tuple-element.30), channel_id=1, source_target_pairs={{112,0},{120,8},{128,16},{136,24},{144,32},{152,40},{160,48},{168,... | collective-permute-start | bytes 196616 | tf_op jit(solution)/shard_map/ppermute | solution.py:20
  67.8 1.9 %collective-permute-start.15 = (bf16[128,256]{0,1:T(8,128)(2,1)S(1)}, bf16[128,256]{0,1:T(8,128)(2,1)S(1)}, u32[]{:S(2)}, u32[]{:S(2)}) collective-permute-start(bf16[128,256]{0,1:T(8,128)(2,1)S(1)} %get-tuple-element.31), channel_id=1, source_target_pairs={{96,0},{104,8},{112,16},{120,24},{128,32},{136,40},{144,48},{152,5... | collective-permute-start | bytes 196616 | tf_op jit(solution)/shard_map/ppermute | solution.py:20
  69.8 1.9 %collective-permute-start.14 = (bf16[128,256]{0,1:T(8,128)(2,1)}, bf16[128,256]{0,1:T(8,128)(2,1)}, u32[]{:S(2)}, u32[]{:S(2)}) collective-permute-start(bf16[128,256]{0,1:T(8,128)(2,1)} %get-tuple-element.32), channel_id=1, source_target_pairs={{80,0},{88,8},{96,16},{104,24},{112,32},{120,40},{128,48},{136,56}... | collective-permute-start | bytes 196616 | tf_op jit(solution)/shard_map/ppermute | solution.py:20
  71.7 1.9 %collective-permute-start.13 = (bf16[128,256]{0,1:T(8,128)(2,1)S(1)}, bf16[128,256]{0,1:T(8,128)(2,1)}, u32[]{:S(2)}, u32[]{:S(2)}) collective-permute-start(bf16[128,256]{0,1:T(8,128)(2,1)S(1)} %get-tuple-element.33), channel_id=1, source_target_pairs={{64,0},{72,8},{80,16},{88,24},{96,32},{104,40},{112,48},{120,56},{... | collective-permute-start | bytes 196616 | tf_op jit(solution)/shard_map/ppermute | solution.py:20
  73.6 3.9 %collective-permute-start.12 = (bf16[128,256]{0,1:T(8,128)(2,1)S(1)}, bf16[128,256]{0,1:T(8,128)(2,1)}, u32[]{:S(2)}, u32[]{:S(2)}) collective-permute-start(bf16[128,256]{0,1:T(8,128)(2,1)S(1)} %get-tuple-element.34), channel_id=1, source_target_pairs={{48,0},{56,8},{64,16},{72,24},{80,32},{88,40},{96,48},{104,56},{11... | collective-permute-start | bytes 196616 | tf_op jit(solution)/shard_map/ppermute | solution.py:20
  77.6 1.9 %collective-permute-start.11 = (bf16[128,256]{0,1:T(8,128)(2,1)S(1)}, bf16[128,256]{0,1:T(8,128)(2,1)}, u32[]{:S(2)}, u32[]{:S(2)}) collective-permute-start(bf16[128,256]{0,1:T(8,128)(2,1)S(1)} %get-tuple-element.35), channel_id=1, source_target_pairs={{32,0},{40,8},{48,16},{56,24},{64,32},{72,40},{80,48},{88,56},{96,... | collective-permute-start | bytes 196616 | tf_op jit(solution)/shard_map/ppermute | solution.py:20
  80.1 2.9 %collective-permute-start.10 = (bf16[128,256]{0,1:T(8,128)(2,1)S(1)}, bf16[128,256]{0,1:T(8,128)(2,1)}, u32[]{:S(2)}, u32[]{:S(2)}) collective-permute-start(bf16[128,256]{0,1:T(8,128)(2,1)S(1)} %get-tuple-element.28), channel_id=1, source_target_pairs={{16,0},{24,8},{32,16},{40,24},{48,32},{56,40},{64,48},{72,56},{80,... | collective-permute-start | bytes 196616 | tf_op jit(solution)/shard_map/ppermute | solution.py:20
  84.5 3.7 %collective-permute-done.11 = bf16[128,256]{0,1:T(8,128)(2,1)} collective-permute-done((bf16[128,256]{0,1:T(8,128)(2,1)S(1)}, bf16[128,256]{0,1:T(8,128)(2,1)}, u32[]{:S(2)}, u32[]{:S(2)}) %collective-permute-start.11) | collective-permute-done | bytes 65568 | tf_op jit(solution)/shard_map/ppermute | solution.py:20
  94.2 4.6 %constant_dynamic-slice_fusion.6 = (bf16[128,1,1024]{2,1,0:T(2,128)(2,1)S(1)}, bf16[128,1,1024]{2,1,0:T(2,128)(2,1)S(1)}, bf16[128,1,1024]{2,1,0:T(2,128)(2,1)S(...) fusion(bf16[128,8,1024]{2,1,0:T(8,128)(2,1)S(1)} %bitcast.91, ...), kind=kLoop, calls=%fused_computation.101 | loop fusion | bytes 4194336 | tf_op jit(solution)/shard_map/jit(_take) | solution.py:122
  98.9 4.6 %collective-permute-start.24 = (bf16[128,1024]{1,0:T(8,128)(2,1)S(1)}, bf16[128,1024]{1,0:T(8,128)(2,1)S(1)}, u32[]{:S(2)}, u32[]{:S(2)}) collective-permute-start(bf16[128,1024]{1,0:T(8,128)(2,1)S(1)} %fusion.34), channel_id=1, source_target_pairs={{0,7},{1,0},{2,1},{3,2},{4,3},{5,4},{6,5},{7,6},{8,15},{9,8},{10,9... | collective-permute-start | bytes 786440 | tf_op jit(solution)/shard_map/ppermute | solution.py:126
  104.6 1.6 %collective-permute-start.22 = (bf16[128,1024]{1,0:T(8,128)(2,1)S(1)}, bf16[128,1024]{1,0:T(8,128)(2,1)}, u32[]{:S(2)}, u32[]{:S(2)}) collective-permute-start(bf16[128,1024]{1,0:T(8,128)(2,1)S(1)} %fusion.36), channel_id=1, source_target_pairs={{0,5},{1,6},{2,7},{3,0},{4,1},{5,2},{6,3},{7,4},{8,13},{9,14},{10,... | collective-permute-start | bytes 786440 | tf_op jit(solution)/shard_map/ppermute | solution.py:126
  107.0 2.3 %collective-permute-start.21 = (bf16[128,1024]{1,0:T(8,128)(2,1)}, bf16[128,1024]{1,0:T(8,128)(2,1)}, u32[]{:S(2)}, u32[]{:S(2)}) collective-permute-start(bf16[128,1024]{1,0:T(8,128)(2,1)} %fusion.37), channel_id=1, source_target_pairs={{0,4},{1,5},{2,6},{3,7},{4,0},{5,1},{6,2},{7,3},{8,12},{9,13},{10,... | collective-permute-start | bytes 786440 | tf_op jit(solution)/shard_map/ppermute | solution.py:126
  112.4 5.2 %collective-permute-done.24 = bf16[128,1024]{1,0:T(8,128)(2,1)S(1)} collective-permute-done((bf16[128,1024]{1,0:T(8,128)(2,1)S(1)}, bf16[128,1024]{1,0:T(8,128)(2,1)S(1)}, u32[]{:S(2)}, u32[]{:S(2)}) %collective-permute-start.24) | collective-permute-done | bytes 262176 | tf_op jit(solution)/shard_map/ppermute | solution.py:126
  117.6 6.4 %collective-permute-start.18 = (bf16[128,1024]{1,0:T(8,128)(2,1)}, bf16[128,1024]{1,0:T(8,128)(2,1)}, u32[]{:S(2)}, u32[]{:S(2)}) collective-permute-start(bf16[128,1024]{1,0:T(8,128)(2,1)} %fusion.40), channel_id=1, source_target_pairs={{0,1},{1,2},{2,3},{3,4},{4,5},{5,6},{6,7},{7,0},{8,9},{9,10},{10,1... | collective-permute-start | bytes 786440 | tf_op jit(solution)/shard_map/ppermute | solution.py:126
  127.9 3.1 %collective-permute-done.19 = bf16[128,1024]{1,0:T(8,128)(2,1)} collective-permute-done((bf16[128,1024]{1,0:T(8,128)(2,1)}, bf16[128,1024]{1,0:T(8,128)(2,1)}, u32[]{:S(2)}, u32[]{:S(2)}) %collective-permute-start.19) | collective-permute-done | bytes 262176 | tf_op jit(solution)/shard_map/ppermute | solution.py:126
  131.0 3.7 %collective-permute-done.18 = bf16[128,1024]{1,0:T(8,128)(2,1)} collective-permute-done((bf16[128,1024]{1,0:T(8,128)(2,1)}, bf16[128,1024]{1,0:T(8,128)(2,1)}, u32[]{:S(2)}, u32[]{:S(2)}) %collective-permute-start.18) | collective-permute-done | bytes 262176 | tf_op jit(solution)/shard_map/ppermute | solution.py:126
  134.7 2.6 %add_convert_fusion = bf16[128,1024]{1,0:T(8,128)(2,1)} fusion(bf16[128,1024]{1,0:T(8,128)(2,1)} %copy-done.8, bf16[128,1024]{1,0:T(8,128)(2,1)} %copy-done.9, bf16[128,1024]{1,0:T(8,128)(2,1)} %collective-permute-done.22, bf16[128,1024]{1,0:T(8,128)(2,1)} %collective-permute-done.21, bf16[128,1024]{1,0:T(8,128)(2,1)} %collective-permute-done.20, ...), kind=kLoop, calls=%fused_computation.43 | loop fusion | flops 2228224 | bytes 2359297 | tf_op jit(solution)/shard_map/convert_element_type | solution.py:127
  (116 shorter events, 38.9 us)
Async XLA Ops:
  0.6 89.8 %copy-start = (bf16[8192,128]{1,0:T(8,128)(2,1)S(1)}, bf16[8192,128]{1,0:T(8,128)(2,1)}, u32[]{:S(2)}) copy-start(bf16[8192,128]{1,0:T(8,128)(2,1)} %param.14) | copy-start | bytes 6291460
  0.6 23.7 %copy-start.14 = (s32[2176]{0:T(1024)S(1)}, s32[2176]{0:T(1024)}, u32[]{:S(2)}) copy-start(s32[2176]{0:T(1024)} %constant.87.clone.1) | copy-start | bytes 26116
  0.7 23.5 %copy-start.7 = (bf16[128,1024]{1,0:T(8,128)(2,1)S(1)}, bf16[128,1024]{1,0:T(8,128)(2,1)}, u32[]{:S(2)}) copy-start(bf16[128,1024]{1,0:T(8,128)(2,1)} %param.9) | copy-start | bytes 786436
  3.6 20.8 %collective-permute-start = (bf16[128,256]{1,0:T(8,128)(2,1)S(1)}, bf16[128,256]{1,0:T(8,128)(2,1)S(1)}, u32[]{:S(2)}, u32[]{:S(2)}) collective-permute-start(bf16[128,256]{1,0:T(8,128)(2,1)S(1)} %get-tuple-element.55), channel_id=1, source_target_pairs={{0,16},{8,24},{16,32},{24,40},{32,48},{40,56},{48,64},{56,72},{64,... | collective-permute-start | bytes 196616 | tf_op jit(solution)/shard_map/ppermute | solution.py:20
  7.4 19.5 %collective-permute-start.1 = (bf16[128,256]{1,0:T(8,128)(2,1)S(1)}, bf16[128,256]{1,0:T(8,128)(2,1)S(1)}, u32[]{:S(2)}, u32[]{:S(2)}) collective-permute-start(bf16[128,256]{1,0:T(8,128)(2,1)S(1)} %get-tuple-element.55), channel_id=1, source_target_pairs={{0,32},{8,40},{16,48},{24,56},{32,64},{40,72},{48,80},{56,88},{64,... | collective-permute-start | bytes 196616 | tf_op jit(solution)/shard_map/ppermute | solution.py:20
  12.6 16.9 %collective-permute-start.2 = (bf16[128,256]{1,0:T(8,128)(2,1)S(1)}, bf16[128,256]{1,0:T(8,128)(2,1)S(1)}, u32[]{:S(2)}, u32[]{:S(2)}) collective-permute-start(bf16[128,256]{1,0:T(8,128)(2,1)S(1)} %get-tuple-element.55), channel_id=1, source_target_pairs={{0,48},{8,56},{16,64},{24,72},{32,80},{40,88},{48,96},{56,104},{64... | collective-permute-start | bytes 196616 | tf_op jit(solution)/shard_map/ppermute | solution.py:20
  18.6 12.9 %collective-permute-start.3 = (bf16[128,256]{1,0:T(8,128)(2,1)S(1)}, bf16[128,256]{1,0:T(8,128)(2,1)S(1)}, u32[]{:S(2)}, u32[]{:S(2)}) collective-permute-start(bf16[128,256]{1,0:T(8,128)(2,1)S(1)} %get-tuple-element.55), channel_id=1, source_target_pairs={{0,64},{8,72},{16,80},{24,88},{32,96},{40,104},{48,112},{56,120},{... | collective-permute-start | bytes 196616 | tf_op jit(solution)/shard_map/ppermute | solution.py:20
  20.9 12.7 %collective-permute-start.4 = (bf16[128,256]{1,0:T(8,128)(2,1)S(1)}, bf16[128,256]{1,0:T(8,128)(2,1)S(1)}, u32[]{:S(2)}, u32[]{:S(2)}) collective-permute-start(bf16[128,256]{1,0:T(8,128)(2,1)S(1)} %get-tuple-element.55), channel_id=1, source_target_pairs={{0,80},{8,88},{16,96},{24,104},{32,112},{40,120},{48,128},{56,136}... | collective-permute-start | bytes 196616 | tf_op jit(solution)/shard_map/ppermute | solution.py:20
  24.4 12.1 %collective-permute-start.5 = (bf16[128,256]{1,0:T(8,128)(2,1)S(1)}, bf16[128,256]{1,0:T(8,128)(2,1)S(1)}, u32[]{:S(2)}, u32[]{:S(2)}) collective-permute-start(bf16[128,256]{1,0:T(8,128)(2,1)S(1)} %get-tuple-element.55), channel_id=1, source_target_pairs={{0,96},{8,104},{16,112},{24,120},{32,128},{40,136},{48,144},{56,15... | collective-permute-start | bytes 196616 | tf_op jit(solution)/shard_map/ppermute | solution.py:20
  26.9 10.2 %collective-permute-start.6 = (bf16[128,256]{1,0:T(8,128)(2,1)S(1)}, bf16[128,256]{1,0:T(8,128)(2,1)S(1)}, u32[]{:S(2)}, u32[]{:S(2)}) collective-permute-start(bf16[128,256]{1,0:T(8,128)(2,1)S(1)} %get-tuple-element.55), channel_id=1, source_target_pairs={{0,112},{8,120},{16,128},{24,136},{32,144},{40,152},{48,160},{56,1... | collective-permute-start | bytes 196616 | tf_op jit(solution)/shard_map/ppermute | solution.py:20
  28.9 11.4 %copy-start.15 = (s32[128]{0:T(128)S(1)}, s32[128]{0:T(128)}, u32[]{:S(2)}) copy-start(s32[128]{0:T(128)} %param.15) | copy-start | bytes 1540
  29.5 8.9 %collective-permute-start.7 = (bf16[128,256]{1,0:T(8,128)(2,1)S(1)}, bf16[128,256]{1,0:T(8,128)(2,1)S(1)}, u32[]{:S(2)}, u32[]{:S(2)}) collective-permute-start(bf16[128,256]{1,0:T(8,128)(2,1)S(1)} %get-tuple-element.55), channel_id=1, source_target_pairs={{0,128},{8,136},{16,144},{24,152},{32,160},{40,168},{48,176},{56,1... | collective-permute-start | bytes 196616 | tf_op jit(solution)/shard_map/ppermute | solution.py:20
  40.2 2.0 %collective-permute-start.8 = (bf16[1024,256]{1,0:T(8,128)(2,1)S(1)}, bf16[1024,256]{1,0:T(8,128)(2,1)S(1)}, u32[]{:S(2)}, u32[]{:S(2)}) collective-permute-start(bf16[1024,256]{1,0:T(8,128)(2,1)S(1)} %constant_dynamic-slice_fusion.8), channel_id=1, source_target_pairs={{0,8},{8,0},{16,24},{24,16},{32,40},{40,32},{48,56},{56,48},{64,72... | collective-permute-start | bytes 1572872 | tf_op jit(solution)/shard_map/ppermute | solution.py:40
  59.7 2.0 %collective-permute-start.9 = (bf16[1024,256]{0,1:T(8,128)(2,1)S(1)}, bf16[1024,256]{0,1:T(8,128)(2,1)S(1)}, u32[]{:S(2)}, u32[]{:S(2)}) collective-permute-start(bf16[1024,256]{0,1:T(8,128)(2,1)S(1)} %fusion.33), channel_id=1, source_target_pairs={{0,8},{8,0},{16,24},{24,16},{32,40},{40,32},{48,56},{56,48},{64,72... | collective-permute-start | bytes 1572872 | tf_op jit(solution)/shard_map/ppermute | solution.py:97
  62.6 11.0 %collective-permute-start.17 = (bf16[128,256]{0,1:T(8,128)(2,1)S(1)}, bf16[128,256]{0,1:T(8,128)(2,1)}, u32[]{:S(2)}, u32[]{:S(2)}) collective-permute-start(bf16[128,256]{0,1:T(8,128)(2,1)S(1)} %get-tuple-element.29), channel_id=1, source_target_pairs={{128,0},{136,8},{144,16},{152,24},{160,32},{168,40},{176,48},{184,... | collective-permute-start | bytes 196616 | tf_op jit(solution)/shard_map/ppermute | solution.py:20
  65.9 11.6 %collective-permute-start.16 = (bf16[128,256]{0,1:T(8,128)(2,1)S(1)}, bf16[128,256]{0,1:T(8,128)(2,1)S(1)}, u32[]{:S(2)}, u32[]{:S(2)}) collective-permute-start(bf16[128,256]{0,1:T(8,128)(2,1)S(1)} %get-tuple-element.30), channel_id=1, source_target_pairs={{112,0},{120,8},{128,16},{136,24},{144,32},{152,40},{160,48},{168,... | collective-permute-start | bytes 196616 | tf_op jit(solution)/shard_map/ppermute | solution.py:20
  67.8 11.7 %collective-permute-start.15 = (bf16[128,256]{0,1:T(8,128)(2,1)S(1)}, bf16[128,256]{0,1:T(8,128)(2,1)S(1)}, u32[]{:S(2)}, u32[]{:S(2)}) collective-permute-start(bf16[128,256]{0,1:T(8,128)(2,1)S(1)} %get-tuple-element.31), channel_id=1, source_target_pairs={{96,0},{104,8},{112,16},{120,24},{128,32},{136,40},{144,48},{152,5... | collective-permute-start | bytes 196616 | tf_op jit(solution)/shard_map/ppermute | solution.py:20
  69.8 14.8 %collective-permute-start.14 = (bf16[128,256]{0,1:T(8,128)(2,1)}, bf16[128,256]{0,1:T(8,128)(2,1)}, u32[]{:S(2)}, u32[]{:S(2)}) collective-permute-start(bf16[128,256]{0,1:T(8,128)(2,1)} %get-tuple-element.32), channel_id=1, source_target_pairs={{80,0},{88,8},{96,16},{104,24},{112,32},{120,40},{128,48},{136,56}... | collective-permute-start | bytes 196616 | tf_op jit(solution)/shard_map/ppermute | solution.py:20
  71.7 12.8 %collective-permute-start.13 = (bf16[128,256]{0,1:T(8,128)(2,1)S(1)}, bf16[128,256]{0,1:T(8,128)(2,1)}, u32[]{:S(2)}, u32[]{:S(2)}) collective-permute-start(bf16[128,256]{0,1:T(8,128)(2,1)S(1)} %get-tuple-element.33), channel_id=1, source_target_pairs={{64,0},{72,8},{80,16},{88,24},{96,32},{104,40},{112,48},{120,56},{... | collective-permute-start | bytes 196616 | tf_op jit(solution)/shard_map/ppermute | solution.py:20
  73.6 10.9 %collective-permute-start.12 = (bf16[128,256]{0,1:T(8,128)(2,1)S(1)}, bf16[128,256]{0,1:T(8,128)(2,1)}, u32[]{:S(2)}, u32[]{:S(2)}) collective-permute-start(bf16[128,256]{0,1:T(8,128)(2,1)S(1)} %get-tuple-element.34), channel_id=1, source_target_pairs={{48,0},{56,8},{64,16},{72,24},{80,32},{88,40},{96,48},{104,56},{11... | collective-permute-start | bytes 196616 | tf_op jit(solution)/shard_map/ppermute | solution.py:20
  77.6 10.7 %collective-permute-start.11 = (bf16[128,256]{0,1:T(8,128)(2,1)S(1)}, bf16[128,256]{0,1:T(8,128)(2,1)}, u32[]{:S(2)}, u32[]{:S(2)}) collective-permute-start(bf16[128,256]{0,1:T(8,128)(2,1)S(1)} %get-tuple-element.35), channel_id=1, source_target_pairs={{32,0},{40,8},{48,16},{56,24},{64,32},{72,40},{80,48},{88,56},{96,... | collective-permute-start | bytes 196616 | tf_op jit(solution)/shard_map/ppermute | solution.py:20
  80.1 9.1 %collective-permute-start.10 = (bf16[128,256]{0,1:T(8,128)(2,1)S(1)}, bf16[128,256]{0,1:T(8,128)(2,1)}, u32[]{:S(2)}, u32[]{:S(2)}) collective-permute-start(bf16[128,256]{0,1:T(8,128)(2,1)S(1)} %get-tuple-element.28), channel_id=1, source_target_pairs={{16,0},{24,8},{32,16},{40,24},{48,32},{56,40},{64,48},{72,56},{80,... | collective-permute-start | bytes 196616 | tf_op jit(solution)/shard_map/ppermute | solution.py:20
  92.7 31.3 %slice-start.3 = ((s8[4456448]{0:T(1024)(128)(4,1)}), s8[4194304]{0:T(1024)(128)(4,1)S(1)}, s32[]{:S(2)}) async-start(s8[4456448]{0:T(1024)(128)(4,1)} %bitcast.89), calls=%async_computation.3 | async-start | bytes 8388608
  94.2 29.8 %slice-start.4 = ((s8[4456448]{0:T(1024)(128)(4,1)}), s8[262144]{0:T(1024)(128)(4,1)S(1)}, s32[]{:S(2)}) async-start(s8[4456448]{0:T(1024)(128)(4,1)} %bitcast.89), calls=%async_computation.4 | async-start | bytes 524288
  98.9 18.6 %collective-permute-start.24 = (bf16[128,1024]{1,0:T(8,128)(2,1)S(1)}, bf16[128,1024]{1,0:T(8,128)(2,1)S(1)}, u32[]{:S(2)}, u32[]{:S(2)}) collective-permute-start(bf16[128,1024]{1,0:T(8,128)(2,1)S(1)} %fusion.34), channel_id=1, source_target_pairs={{0,7},{1,0},{2,1},{3,2},{4,3},{5,4},{6,5},{7,6},{8,15},{9,8},{10,9... | collective-permute-start | bytes 786440 | tf_op jit(solution)/shard_map/ppermute | solution.py:126
  103.6 13.9 %collective-permute-start.23 = (bf16[128,1024]{1,0:T(8,128)(2,1)S(1)}, bf16[128,1024]{1,0:T(8,128)(2,1)S(1)}, u32[]{:S(2)}, u32[]{:S(2)}) collective-permute-start(bf16[128,1024]{1,0:T(8,128)(2,1)S(1)} %fusion.35), channel_id=1, source_target_pairs={{0,6},{1,7},{2,0},{3,1},{4,2},{5,3},{6,4},{7,5},{8,14},{9,15},{10,... | collective-permute-start | bytes 786440 | tf_op jit(solution)/shard_map/ppermute | solution.py:126
  104.6 22.6 %collective-permute-start.22 = (bf16[128,1024]{1,0:T(8,128)(2,1)S(1)}, bf16[128,1024]{1,0:T(8,128)(2,1)}, u32[]{:S(2)}, u32[]{:S(2)}) collective-permute-start(bf16[128,1024]{1,0:T(8,128)(2,1)S(1)} %fusion.36), channel_id=1, source_target_pairs={{0,5},{1,6},{2,7},{3,0},{4,1},{5,2},{6,3},{7,4},{8,13},{9,14},{10,... | collective-permute-start | bytes 786440 | tf_op jit(solution)/shard_map/ppermute | solution.py:126
  107.0 20.1 %collective-permute-start.21 = (bf16[128,1024]{1,0:T(8,128)(2,1)}, bf16[128,1024]{1,0:T(8,128)(2,1)}, u32[]{:S(2)}, u32[]{:S(2)}) collective-permute-start(bf16[128,1024]{1,0:T(8,128)(2,1)} %fusion.37), channel_id=1, source_target_pairs={{0,4},{1,5},{2,6},{3,7},{4,0},{5,1},{6,2},{7,3},{8,12},{9,13},{10,... | collective-permute-start | bytes 786440 | tf_op jit(solution)/shard_map/ppermute | solution.py:126
  109.3 14.7 %copy-start.5 = (bf16[2176,256]{1,0:T(8,128)(2,1)S(1)}, bf16[2176,256]{1,0:T(8,128)(2,1)}, u32[]{:S(2)}) copy-start(bf16[2176,256]{1,0:T(8,128)(2,1)} %copy-done.3) | copy-start | bytes 3342340
  110.2 17.8 %collective-permute-start.20 = (bf16[128,1024]{1,0:T(8,128)(2,1)}, bf16[128,1024]{1,0:T(8,128)(2,1)}, u32[]{:S(2)}, u32[]{:S(2)}) collective-permute-start(bf16[128,1024]{1,0:T(8,128)(2,1)} %fusion.38), channel_id=1, source_target_pairs={{0,3},{1,4},{2,5},{3,6},{4,7},{5,0},{6,1},{7,2},{8,11},{9,12},{10,... | collective-permute-start | bytes 786440 | tf_op jit(solution)/shard_map/ppermute | solution.py:126
  117.5 13.4 %collective-permute-start.19 = (bf16[128,1024]{1,0:T(8,128)(2,1)}, bf16[128,1024]{1,0:T(8,128)(2,1)}, u32[]{:S(2)}, u32[]{:S(2)}) collective-permute-start(bf16[128,1024]{1,0:T(8,128)(2,1)} %fusion.39), channel_id=1, source_target_pairs={{0,2},{1,3},{2,4},{3,5},{4,6},{5,7},{6,0},{7,1},{8,10},{9,11},{10,... | collective-permute-start | bytes 786440 | tf_op jit(solution)/shard_map/ppermute | solution.py:126
  117.6 17.1 %collective-permute-start.18 = (bf16[128,1024]{1,0:T(8,128)(2,1)}, bf16[128,1024]{1,0:T(8,128)(2,1)}, u32[]{:S(2)}, u32[]{:S(2)}) collective-permute-start(bf16[128,1024]{1,0:T(8,128)(2,1)} %fusion.40), channel_id=1, source_target_pairs={{0,1},{1,2},{2,3},{3,4},{4,5},{5,6},{6,7},{7,0},{8,9},{9,10},{10,1... | collective-permute-start | bytes 786440 | tf_op jit(solution)/shard_map/ppermute | solution.py:126
  (14 other events, 57.2 us)
